TPU v7x, 32 devices: a whole 2x2x4 slice. The times are simulated.
32 devices in a mesh: ctx: 8 (over z, y), dp: 2 (over x), section: 2 (over core).
Axes of the slice: x: 2, y: 2, z: 4, core: 2. Of those that a mesh axis runs over, the one named last changes fastest.
Arguments:
- normed: bfloat16 [2, 3072, 1024], P('dp', 'ctx'), may hold values from -40 to 40
- w_query: bfloat16 [1024, 1024], P('dp', 'section'), may hold values from -0.1875 to 0.1875
- w_key: bfloat16 [1024, 1024], P('dp', 'section'), may hold values from -0.28125 to 0.28125
- w_value: bfloat16 [1024, 1024], P('dp', 'section'), may hold values from -0.1875 to 0.1875
- block_mask: int32 [24, 7], replicated, may hold values from 0 to 1, as said below
- cotangent: bfloat16 [2, 3072, 1024], P('dp', 'ctx', 'section'), may hold values from -8 to 8
Outputs:
- attended: bfloat16 [2, 3072, 1024], P('dp', 'ctx', 'section')
- grad_input: bfloat16 [2, 3072, 1024], P('dp', 'ctx')
- grad_weights: float32 [1024, 3, 1024], P(('ctx', 'dp'), None, 'section')
Inputs may be any that keep to these rules, and one draw needn't show every extreme that they name: `block_mask`: every row has a 1 in column 3; no row names a key block outside 0 to 23; a row holds at most 5 ones, and some row holds exactly 5.
All inputs are finite; a program needn't handle non-finite values.
Results may differ from a plain program's by a relative error of at most 0.014.
The roundings to bfloat16 on the way count: a program that leaves them out, or rounds other values in their place, can miss the bound.
Values may be sent and summed in bfloat16 or wider, within the bound.
No kernel may reach another device: no remote copies, remote signals or barrier semaphores. Data moves between devices by JAX's collectives and lax.ppermute only.
A program may use at most 64 MiB of HBM per device.

v0:
```python
import jax
import jax.numpy as jnp
from jax import lax
from jax.sharding import PartitionSpec as P

HD = 64
BLOCK = 128
REACH = 3


def extended(cells, sides, width):
    for axis, dim in sides:
        count = lax.axis_size(axis)
        ends = count - 1
        head = lax.slice_in_dim(cells, 0, width, axis=dim)
        tail = lax.slice_in_dim(cells, cells.shape[dim] - width, cells.shape[dim], axis=dim)
        cells = jnp.concatenate(
            [
                lax.ppermute(tail, axis, [(i, (i + 1) % count) for i in range(ends)]),
                cells,
                lax.ppermute(head, axis, [((i + 1) % count, i) for i in range(ends)]),
            ],
            axis=dim,
        )
    return cells


def shifted(value, axis, steps):
    count = lax.axis_size(axis)
    leading, last = (max(0, -steps), min(count, count - steps))
    return lax.ppermute(value, axis, [(source, source + steps) for source in range(leading, last)])


def attend(query_block, key_window, seen_slots, score_scale):
    scores = (
        jnp.einsum("qhd,skhd->hqsk", query_block, key_window, preferred_element_type=jnp.float32)
        * score_scale
    )
    is_seen = seen_slots[None, None, :, None] > 0
    row_top = jnp.max(jnp.where(is_seen, scores, -jnp.inf), axis=(2, 3), keepdims=True)
    raised = jnp.where(is_seen, jnp.exp(scores - row_top), 0.0)
    row_total = jnp.sum(raised, axis=(2, 3), keepdims=True)
    return (raised / row_total, row_top, row_total)


def per_device(normed, w_query, w_key, w_value, block_mask, cotangent):
    tokens = normed[0]
    upstream = cotangent[0]
    length = tokens.shape[0]
    features = upstream.shape[1]
    head_count = features // HD
    blocks = length // BLOCK
    frame_len = blocks + 2 * REACH
    span_len = 2 * REACH + 1
    score_scale = HD ** (-0.5)
    query_full, key_full, value_full = (
        lax.all_gather(w_query, "dp", axis=0, tiled=True),
        lax.all_gather(w_key, "dp", axis=0, tiled=True),
        lax.all_gather(w_value, "dp", axis=0, tiled=True),
    )
    queries = jnp.dot(tokens, query_full, preferred_element_type=jnp.float32).astype(jnp.bfloat16)
    key_rows = jnp.dot(tokens, key_full, preferred_element_type=jnp.float32).astype(jnp.bfloat16)
    value_rows = jnp.dot(tokens, value_full, preferred_element_type=jnp.float32).astype(
        jnp.bfloat16
    )
    framed = extended(jnp.stack([key_rows, value_rows]), (("ctx", 1),), REACH * BLOCK)
    framed = framed.reshape(2, frame_len, BLOCK, head_count, HD)
    query_blocks = queries.reshape(blocks, BLOCK, head_count, HD)
    upstream_blocks = upstream.reshape(blocks, BLOCK, head_count, HD)
    first_block = lax.axis_index("ctx") * blocks
    padded_mask = jnp.pad(block_mask, ((REACH, REACH), (0, 0)))
    frame_mask = lax.dynamic_slice(padded_mask, (first_block, 0), (frame_len, span_len))
    own_mask = frame_mask[REACH : REACH + blocks]
    positions = jnp.arange(span_len, dtype=jnp.int32)
    slot_order = jnp.broadcast_to(positions[None, :], (blocks, span_len))
    slot_index = slot_order + jnp.arange(blocks, dtype=jnp.int32)[:, None]

    def windows(block_at):
        picked = lax.dynamic_slice_in_dim(framed, block_at, span_len, 1)
        return (picked[0], picked[1])

    def forward(running, block_at):
        query_block = lax.dynamic_index_in_dim(query_blocks, block_at, 0, False)
        key_window, value_window = windows(block_at)
        seen_slots = lax.dynamic_index_in_dim(own_mask, block_at, 0, False)
        probability, row_top, row_total = attend(query_block, key_window, seen_slots, score_scale)
        mixed_out = jnp.einsum(
            "hqsk,skhd->qhd",
            probability.astype(jnp.bfloat16),
            value_window,
            preferred_element_type=jnp.float32,
        ).astype(jnp.bfloat16)
        return (running, (mixed_out, row_top[:, :, 0, 0], row_total[:, :, 0, 0]))

    block_ids = jnp.arange(blocks, dtype=jnp.int32)
    _, (mixed_outs, row_tops, row_totals) = lax.scan(forward, jnp.zeros((), jnp.float32), block_ids)
    attended = mixed_outs.reshape(1, length, features)

    def backward(running, block_at):
        query_block = lax.dynamic_index_in_dim(query_blocks, block_at, 0, False)
        upstream_block = lax.dynamic_index_in_dim(upstream_blocks, block_at, 0, False)
        key_window, value_window = windows(block_at)
        seen_slots = lax.dynamic_index_in_dim(own_mask, block_at, 0, False)
        probability, _, _ = attend(query_block, key_window, seen_slots, score_scale)
        weights = probability.astype(jnp.bfloat16)
        prob_grad = jnp.einsum(
            "qhd,skhd->hqsk", upstream_block, value_window, preferred_element_type=jnp.float32
        )
        row_delta = jnp.sum(probability * prob_grad, axis=(2, 3), keepdims=True)
        score_grad = (probability * (prob_grad - row_delta)).astype(jnp.bfloat16)
        query_grad = (
            score_scale
            * jnp.einsum(
                "hqsk,skhd->qhd", score_grad, key_window, preferred_element_type=jnp.float32
            )
        ).astype(jnp.bfloat16)
        key_part = score_scale * jnp.einsum(
            "hqsk,qhd->skhd", score_grad, query_block, preferred_element_type=jnp.float32
        )
        value_part = jnp.einsum(
            "hqsk,qhd->skhd", weights, upstream_block, preferred_element_type=jnp.float32
        )
        slot_rows = lax.dynamic_index_in_dim(slot_index, block_at, 0, False)
        running = running.at[0, slot_rows].add(key_part).at[1, slot_rows].add(value_part)
        return (running, (query_grad, row_delta[:, :, 0, 0]))

    start_state = jnp.zeros((2, frame_len, BLOCK, head_count, HD), jnp.float32)
    frame_grads, (query_grads, row_deltas) = lax.scan(backward, start_state, block_ids)
    query_grad = query_grads.reshape(length, features)
    frame_grads = frame_grads.reshape(2, frame_len, BLOCK, features)
    left_side = frame_grads[:, :REACH]
    right_side = frame_grads[:, blocks + REACH :]
    middle = frame_grads[:, REACH : REACH + blocks]
    for offset in (1, -1):
        outgoing = right_side if offset == 1 else left_side
        arrived = shifted(outgoing.astype(jnp.bfloat16), "ctx", offset).astype(outgoing.dtype)
        if offset == 1:
            middle = middle.at[:, :REACH].add(arrived)
        else:
            middle = middle.at[:, blocks - REACH :].add(arrived)
    key_grad = middle[0].reshape(length, features).astype(jnp.bfloat16)
    value_grad = middle[1].reshape(length, features).astype(jnp.bfloat16)
    contract = (((1,), (1,)), ((), ()))
    partial_input = (
        lax.dot_general(query_grad, query_full, contract, preferred_element_type=jnp.float32)
        + lax.dot_general(key_grad, key_full, contract, preferred_element_type=jnp.float32)
        + lax.dot_general(value_grad, value_full, contract, preferred_element_type=jnp.float32)
    )
    grad_input = lax.psum(partial_input.astype(jnp.bfloat16), "section")[None]
    grads_all = jnp.stack([query_grad, key_grad, value_grad], axis=1)
    group_part = lax.psum_scatter(
        jnp.einsum("tr,tcf->rcf", tokens, grads_all, preferred_element_type=jnp.float32).astype(
            jnp.bfloat16
        ),
        "ctx",
        scatter_dimension=0,
        tiled=True,
    )
    summed = lax.psum_scatter(group_part, "dp", scatter_dimension=0, tiled=True).astype(jnp.float32)
    grad_weights = summed / lax.axis_size("dp")
    return (attended, grad_input, grad_weights)


def solution(mesh):
    in_specs = (
        P("dp", "ctx", None),
        P("dp", "section"),
        P("dp", "section"),
        P("dp", "section"),
        P(),
        P("dp", "ctx", "section"),
    )
    out_specs = (P("dp", "ctx", "section"), P("dp", "ctx", None), P(("ctx", "dp"), None, "section"))
    return jax.shard_map(
        per_device, mesh=mesh, in_specs=in_specs, out_specs=out_specs, check_vma=False
    )
```

profile of v0, /device:TPU:0, one launch (start us, length us, event | category | flops | bytes accessed | tf_op | source)
XLA Modules:
  0.0 379.1 jit_solution(11920346828465409349)
XLA Ops:
  9.5 24.1 %all-gather.6.cloned.1.call-done = bf16[1024,512]{1,0:T(8,128)(2,1)} async-done(((bf16[512,512]{1,0:T(8,128)(2,1)}), bf16[1024,512]{1,0:T(8,128)(2,1)}) %all-gather.6.cloned.1.call-update) | async-done | bytes 1048592 | tf_op jit(solution)/shard_map/all_gather | solution.py:59
  35.4 21.1 %all-gather.4.cloned.1.call-done = bf16[1024,512]{1,0:T(8,128)(2,1)} async-done(((bf16[512,512]{1,0:T(8,128)(2,1)}), bf16[1024,512]{1,0:T(8,128)(2,1)}) %all-gather.4.cloned.1.call-update) | async-done | bytes 1048592 | tf_op jit(solution)/shard_map/all_gather | solution.py:58
  60.4 5.5 %collective-permute-start = (bf16[2,384,512]{2,1,0:T(8,128)(2,1)S(1)}, bf16[2,384,512]{2,1,0:T(8,128)(2,1)}, u32[]{:S(2)}, u32[]{:S(2)}) collective-permute-start(bf16[2,384,512]{2,1,0:T(8,128)(2,1)S(1)} %pad_maximum_fusion.1), channel_id=1, source_target_pairs={{0,4},{4,8},{8,12},{12,16},{16,20},{20,24},{24,28},{1,5},{5,9},{9,... | collective-permute-start | bytes 2359304 | tf_op jit(solution)/shard_map/ppermute | solution.py:19
  68.1 11.2 %all-gather.8.cloned.1.call-done = bf16[1024,512]{1,0:T(8,128)(2,1)} async-done(((bf16[512,512]{1,0:T(8,128)(2,1)}), bf16[1024,512]{1,0:T(8,128)(2,1)}) %all-gather.8.cloned.1.call-update) | async-done | bytes 1048592 | tf_op jit(solution)/shard_map/all_gather | solution.py:57
  82.9 14.1 %collective-permute-done = bf16[2,384,512]{2,1,0:T(8,128)(2,1)} collective-permute-done((bf16[2,384,512]{2,1,0:T(8,128)(2,1)S(1)}, bf16[2,384,512]{2,1,0:T(8,128)(2,1)}, u32[]{:S(2)}, u32[]{:S(2)}) %collective-permute-start) | collective-permute-done | bytes 786464 | tf_op jit(solution)/shard_map/ppermute | solution.py:19
  98.8 4.6 %reshape.200 = bf16[2,9,128,8,64]{4,3,2,1,0:T(8,128)(2,1)} reshape(bf16[2,1152,512]{2,1,0:T(8,128)(2,1)S(1)} %pad_maximum_fusion) | data formatting | bytes 4718592 | tf_op jit(solution)/shard_map/reshape | solution.py:67
  103.3 6.1 %copy.83 = bf16[2,9,128,8,64]{2,4,1,3,0:T(8,128)(2,1)} copy(bf16[2,9,128,8,64]{4,3,2,1,0:T(8,128)(2,1)} %reshape.200) | data formatting | bytes 4718592 | tf_op jit(solution)/shard_map/while | solution.py:96
  109.5 2.8 broadcast_in_dim.61
  112.3 76.9 %while.27 = (s32[]{:T(128)}, f32[2,9,128,8,64]{2,4,3,1,0:T(8,128)}, bf16[3,128,8,64]{1,3,2,0:T(8,128)(2,1)S(1)}, s32[3]{0:T(128)S(1)}, s32[3,7]{1,0:T(4,128)S(1)...) while((s32[]{:T(128)}, f32[2,9,128,8,64]{2,4,3,1,0:T(8,128)}, ...), condition=%wide.region_10.11_spmd, body=%wide.region_4.10_spmd.sunk | while | flops 611644544 | bytes 56669256 | solution.py:128
  121.1 2.6 multiply_reduce_fusion.2
  128.9 4.8 %scatter_fusion = f32[2,9,128,8,64]{2,4,3,1,0:T(8,128)} fusion(f32[2,9,128,8,64]{2,4,3,1,0:T(8,128)} %get-tuple-element.398, s32[7]{0:T(128)S(1)} %select_bitcast_fusion.5, f32[7,128,8,64]{1,3,2,0:T(8,128)} %copy.129), kind=kCustom, calls=%fused_computation.clone.1 | custom fusion | flops 458752 | bytes 5505080 | tf_op jit(solution)/shard_map/while/body/eval_jaxpr/scatter-add | solution.py:124
  133.7 4.3 %scatter_fusion.1 = f32[2,9,128,8,64]{2,4,3,1,0:T(8,128)} fusion(f32[2,9,128,8,64]{2,4,3,1,0:T(8,128)} %scatter_fusion, s32[7]{0:T(128)S(1)} %get-tuple-element.349, f32[7,128,8,64]{1,3,2,0:T(8,128)S(1)} %copy.130), kind=kCustom, calls=%fused_computation.1.clone.1 | custom fusion | flops 458752 | bytes 5505080 | tf_op jit(solution)/shard_map/while/body/eval_jaxpr/scatter-add | solution.py:124
  146.8 2.6 multiply_reduce_fusion.2
  154.6 4.8 %scatter_fusion = f32[2,9,128,8,64]{2,4,3,1,0:T(8,128)} fusion(f32[2,9,128,8,64]{2,4,3,1,0:T(8,128)} %get-tuple-element.398, s32[7]{0:T(128)S(1)} %select_bitcast_fusion.5, f32[7,128,8,64]{1,3,2,0:T(8,128)} %copy.129), kind=kCustom, calls=%fused_computation.clone.1 | custom fusion | flops 458752 | bytes 5505080 | tf_op jit(solution)/shard_map/while/body/eval_jaxpr/scatter-add | solution.py:124
  159.4 4.2 %scatter_fusion.1 = f32[2,9,128,8,64]{2,4,3,1,0:T(8,128)} fusion(f32[2,9,128,8,64]{2,4,3,1,0:T(8,128)} %scatter_fusion, s32[7]{0:T(128)S(1)} %get-tuple-element.349, f32[7,128,8,64]{1,3,2,0:T(8,128)S(1)} %copy.130), kind=kCustom, calls=%fused_computation.1.clone.1 | custom fusion | flops 458752 | bytes 5505080 | tf_op jit(solution)/shard_map/while/body/eval_jaxpr/scatter-add | solution.py:124
  172.4 2.6 multiply_reduce_fusion.2
  180.2 4.8 %scatter_fusion = f32[2,9,128,8,64]{2,4,3,1,0:T(8,128)} fusion(f32[2,9,128,8,64]{2,4,3,1,0:T(8,128)} %get-tuple-element.398, s32[7]{0:T(128)S(1)} %select_bitcast_fusion.5, f32[7,128,8,64]{1,3,2,0:T(8,128)} %copy.129), kind=kCustom, calls=%fused_computation.clone.1 | custom fusion | flops 458752 | bytes 5505080 | tf_op jit(solution)/shard_map/while/body/eval_jaxpr/scatter-add | solution.py:124
  185.0 4.2 %scatter_fusion.1 = f32[2,9,128,8,64]{2,4,3,1,0:T(8,128)} fusion(f32[2,9,128,8,64]{2,4,3,1,0:T(8,128)} %scatter_fusion, s32[7]{0:T(128)S(1)} %get-tuple-element.349, f32[7,128,8,64]{1,3,2,0:T(8,128)S(1)} %copy.130), kind=kCustom, calls=%fused_computation.1.clone.1 | custom fusion | flops 458752 | bytes 5505080 | tf_op jit(solution)/shard_map/while/body/eval_jaxpr/scatter-add | solution.py:124
  189.3 2.9 bitcast_convert_fusion
  192.3 5.4 %collective-permute-start.2 = (bf16[2,3,128,512]{2,3,1,0:T(8,128)(2,1)S(1)}, bf16[2,3,128,512]{2,3,1,0:T(8,128)(2,1)}, u32[]{:S(2)}, u32[]{:S(2)}) collective-permute-start(bf16[2,3,128,512]{2,3,1,0:T(8,128)(2,1)S(1)} %get-tuple-element.236), channel_id=1, source_target_pairs={{0,4},{4,8},{8,12},{12,16},{16,20},{20,24},{24,28},{1,5},{5,9},{9,... | collective-permute-start | bytes 2359304 | tf_op jit(solution)/shard_map/ppermute | solution.py:31
  201.6 29.0 %collective-permute-done.2 = bf16[2,3,128,512]{2,3,1,0:T(8,128)(2,1)} collective-permute-done((bf16[2,3,128,512]{2,3,1,0:T(8,128)(2,1)S(1)}, bf16[2,3,128,512]{2,3,1,0:T(8,128)(2,1)}, u32[]{:S(2)}, u32[]{:S(2)}) %collective-permute-start.2) | collective-permute-done | bytes 786464 | tf_op jit(solution)/shard_map/ppermute | solution.py:31
  230.7 2.1 fusion.41
  233.7 4.5 %convolution_convert_fusion = bf16[3,512,1024]{2,1,0:T(8,128)(2,1)} fusion(bf16[384,1,512]{0,2,1:T(8,128)(2,1)S(1)} %copy.97, bf16[384,1,512]{0,2,1:T(8,128)(2,1)S(1)} %copy.96, bf16[384,1,512]{0,2,1:T(8,128)(2,1)} %stack_reshape.3, bf16[1,384,1024]{2,1,0:T(8,128)(2,1)S(1)} %copy-done), kind=kOutput, calls=%fused_computation.64 | convolution fusion | flops 1210712064 | bytes 5111808 | tf_op jit(solution)/shard_map/tr,tcf->rcf/dot_general | solution.py:152
  238.1 4.7 %copy.120 = bf16[1024,1536]{1,0:T(8,128)(2,1)} copy(bf16[1024,1536]{0,1:T(8,128)(2,1)} %bitcast.204) | data formatting | bytes 6291456
  246.0 71.7 %reduce-scatter.4.cloned.1.call-done = bf16[128,1536]{1,0:T(8,128)(2,1)} async-done(((bf16[1024,1536]{1,0:T(8,128)(2,1)}), bf16[128,1536]{1,0:T(8,128)(2,1)}) %reduce-scatter.4.cloned.1.call-update) | async-done | bytes 393232
  324.0 27.1 %while.26 = (s32[]{:T(128)}, bf16[3,128,8,64]{1,3,2,0:T(8,128)(2,1)S(1)}, s32[3]{0:T(128)S(1)}, bf16[2,9,128,8,64]{2,4,1,3,0:T(8,128)(2,1)}, s32[3,7]{1,0:T(4,12...) while((s32[]{:T(128)}, ...), condition=%wide.region_3.4_spmd, body=%wide.region_0.3_spmd.sunk | while | flops 245954576 | bytes 13128970 | solution.py:96
  330.6 2.4 fusion.82
  339.7 2.4 fusion.82
  345.9 2.1 select_reduce_fusion.4
  348.7 2.4 fusion.82
  354.7 15.5 %all-reduce.7.cloned.1.call-done = bf16[1,384,1024]{2,1,0:T(8,128)(2,1)} async-done(((bf16[1,384,1024]{2,1,0:T(8,128)(2,1)}), bf16[1,384,1024]{2,1,0:T(8,128)(2,1)}) %all-reduce.7.cloned.1.call-update) | async-done | bytes 786448 | tf_op jit(solution)/shard_map/psum | solution.py:149
  370.2 2.1 copy.152
  (123 shorter events, 72.9 us)
Async XLA Ops:
  7.2 26.4 %copy-start = (bf16[1,384,1024]{2,1,0:T(8,128)(2,1)S(1)}, bf16[1,384,1024]{2,1,0:T(8,128)(2,1)}, u32[]{:S(2)}) copy-start(bf16[1,384,1024]{2,1,0:T(8,128)(2,1)} %param.18) | copy-start | bytes 2359300
  7.2 26.4 %all-gather.6.cloned.1.call-start = ((), (), s32[]{:S(2)}) async-start(), calls=%async_computation.2 | async-start | bytes 1572864 | tf_op jit(solution)/shard_map/all_gather | solution.py:59
  7.9 48.6 %all-gather.4.cloned.1.call-start = ((), (), s32[]{:S(2)}) async-start(), calls=%async_computation.1 | async-start | bytes 1572864 | tf_op jit(solution)/shard_map/all_gather | solution.py:58
  8.7 57.2 %copy-start.10 = (s32[24,7]{0,1:T(8,128)S(1)}, s32[24,7]{0,1:T(8,128)}, u32[]{:S(2)}) copy-start(s32[24,7]{0,1:T(8,128)} %param.22) | copy-start | bytes 2020
  8.7 57.3 %copy-start.9 = (bf16[1,384,512]{2,1,0:T(8,128)(2,1)S(1)}, bf16[1,384,512]{2,1,0:T(8,128)(2,1)}, u32[]{:S(2)}) copy-start(bf16[1,384,512]{2,1,0:T(8,128)(2,1)} %param.23) | copy-start | bytes 1179652
  8.7 70.7 %all-gather.8.cloned.1.call-start = ((), (), s32[]{:S(2)}) async-start(), calls=%async_computation.3 | async-start | bytes 1572864 | tf_op jit(solution)/shard_map/all_gather | solution.py:57
  9.4 308.3 %reduce-scatter.4.cloned.1.call-start = ((), (), s32[]{:S(2)}) async-start(), calls=%async_computation.5 | async-start | bytes 3538944
  35.4 30.5 %copy-start.4 = (bf16[1,384,512]{2,1,0:T(8,128)(2,1)}, bf16[1,384,512]{2,1,0:T(8,128)(2,1)S(1)}, u32[]{:S(2)}) copy-start(bf16[1,384,512]{2,1,0:T(8,128)(2,1)S(1)} %fusion.44) | copy-start | bytes 1179652
  58.3 0.7 copy-start.5
  59.1 22.9 %collective-permute-start.1 = (bf16[2,384,512]{2,1,0:T(8,128)(2,1)S(1)}, bf16[2,384,512]{2,1,0:T(8,128)(2,1)S(1)}, u32[]{:S(2)}, u32[]{:S(2)}) collective-permute-start(bf16[2,384,512]{2,1,0:T(8,128)(2,1)S(1)} %pad_maximum_fusion.1), channel_id=1, source_target_pairs={{4,0},{8,4},{12,8},{16,12},{20,16},{24,20},{28,24},{5,1},{9,5},{13... | collective-permute-start | bytes 2359304 | tf_op jit(solution)/shard_map/ppermute | solution.py:21
  60.4 36.6 %collective-permute-start = (bf16[2,384,512]{2,1,0:T(8,128)(2,1)S(1)}, bf16[2,384,512]{2,1,0:T(8,128)(2,1)}, u32[]{:S(2)}, u32[]{:S(2)}) collective-permute-start(bf16[2,384,512]{2,1,0:T(8,128)(2,1)S(1)} %pad_maximum_fusion.1), channel_id=1, source_target_pairs={{0,4},{4,8},{8,12},{12,16},{16,20},{20,24},{24,28},{1,5},{5,9},{9,... | collective-permute-start | bytes 2359304 | tf_op jit(solution)/shard_map/ppermute | solution.py:19
  82.1 0.9 copy-start.8
  109.5 2.9 copy-start.11
  189.3 3.1 copy-start.6
  192.3 38.3 %collective-permute-start.2 = (bf16[2,3,128,512]{2,3,1,0:T(8,128)(2,1)S(1)}, bf16[2,3,128,512]{2,3,1,0:T(8,128)(2,1)}, u32[]{:S(2)}, u32[]{:S(2)}) collective-permute-start(bf16[2,3,128,512]{2,3,1,0:T(8,128)(2,1)S(1)} %get-tuple-element.236), channel_id=1, source_target_pairs={{0,4},{4,8},{8,12},{12,16},{16,20},{20,24},{24,28},{1,5},{5,9},{9,... | collective-permute-start | bytes 2359304 | tf_op jit(solution)/shard_map/ppermute | solution.py:31
  197.7 33.0 %collective-permute-start.3 = (bf16[2,3,128,512]{2,3,1,0:T(8,128)(2,1)S(1)}, bf16[2,3,128,512]{2,3,1,0:T(8,128)(2,1)}, u32[]{:S(2)}, u32[]{:S(2)}) collective-permute-start(bf16[2,3,128,512]{2,3,1,0:T(8,128)(2,1)S(1)} %get-tuple-element.237), channel_id=1, source_target_pairs={{4,0},{8,4},{12,8},{16,12},{20,16},{24,20},{28,24},{5,1},{9,5},{13... | collective-permute-start | bytes 2359304 | tf_op jit(solution)/shard_map/ppermute | solution.py:31
  233.0 5.1 %copy-start.1 = (bf16[1,3,128,512]{3,2,1,0:T(8,128)(2,1)}, bf16[1,3,128,512]{3,2,1,0:T(8,128)(2,1)S(1)}, u32[]{:S(2)}) copy-start(bf16[1,3,128,512]{3,2,1,0:T(8,128)(2,1)S(1)} %copy.91) | copy-start | bytes 1179652
  233.2 4.9 %copy-start.2 = (bf16[1,3,128,512]{3,2,1,0:T(8,128)(2,1)}, bf16[1,3,128,512]{3,2,1,0:T(8,128)(2,1)S(1)}, u32[]{:S(2)}) copy-start(bf16[1,3,128,512]{3,2,1,0:T(8,128)(2,1)S(1)} %copy.92) | copy-start | bytes 1179652
  238.1 4.8 %copy-start.12 = (u32[32]{0:T(128)S(1)}, u32[32]{0:T(128)}, u32[]{:S(2)}) copy-start(u32[32]{0:T(128)} %constant.190) | copy-start | bytes 388
  242.9 109.8 %all-reduce.9.cloned.1.call-start = ((), (), s32[]{:S(2)}) async-start(), calls=%async_computation.6 | async-start | bytes 1048576
  246.0 76.2 %copy-start.3 = (bf16[1,3,128,512]{3,2,1,0:T(8,128)(2,1)S(1)}, bf16[1,3,128,512]{3,2,1,0:T(8,128)(2,1)}, u32[]{:S(2)}) copy-start(bf16[1,3,128,512]{3,2,1,0:T(8,128)(2,1)} %copy-done.2) | copy-start | bytes 1179652
  320.2 50.0 %all-reduce.7.cloned.1.call-start = ((), (), s32[]{:S(2)}) async-start(), calls=%async_computation.4 | async-start | bytes 1572864 | tf_op jit(solution)/shard_map/psum | solution.py:149
  320.2 2.1 copy-start.7
Sparse Core Ops, SparseCore 0:
  9.6 23.9 all-gather.5
  35.1 21.2 all-gather.3
  58.0 21.2 all-gather.7
  243.0 74.6 reduce-scatter.3
  320.3 27.6 all-reduce.8
  350.9 19.2 all-reduce.6
where the time goes:
time: 381 us; the launch traced here: 379 us
  waiting for transfers between devices  189 us (50%)
  matrix products  56 us (15%)
  other arithmetic  43.8 us (11%)
  local copies, waits for them, and re-layouts  41.8 us (11%)
  loops' own time  19.7 us (5%)
  between operations  15.1 us (4%)
  starting transfers between devices  13.9 us (4%)
    unnamed x8, waiting for transfers between devices  73.8 us
    ppermute x2, waiting for transfers between devices, shifted(): lax.ppermute(value, axis, [(source, source + steps) for source in range(l...  29 us
    scatter-add x6, other arithmetic, backward(): running.at[0, slot_rows].add(key_part).at[1, slot_rows].add(value_part)  27.2 us
    all_gather x1, waiting for transfers between devices, per_device(): lax.all_gather(w_value, 'dp', axis=0, tiled=True)  24.1 us
    all_gather x1, waiting for transfers between devices, per_device(): lax.all_gather(w_key, 'dp', axis=0, tiled=True)  21.1 us
    psum x1, waiting for transfers between devices, per_device(): grad_input = lax.psum(partial_input.astype(jnp.bfloat16), 'section')[None]  15.5 us
    ppermute x1, waiting for transfers between devices, extended(): lax.ppermute(tail, axis, [(i, (i + 1) % count) for i in range(ends)])  14.1 us
    unnamed x34, local copies, waits for them, and re-layouts  12.8 us
  transfers between devices with their start and end apart: 10, of which 7 were waited for; matrix products, arithmetic and copies ran while one was open for 10% of the time, Pallas kernels for 0%

commit v1 on v0

--- a/solution.py
+++ b/solution.py
@@ -6,6 +6,7 @@
 HD = 64
 BLOCK = 128
 REACH = 3
+expand_spot = lambda original: lax.all_gather(original, "section").sum(axis=0)
 
 
 def extended(cells, sides, width):
@@ -146,7 +147,7 @@
         + lax.dot_general(key_grad, key_full, contract, preferred_element_type=jnp.float32)
         + lax.dot_general(value_grad, value_full, contract, preferred_element_type=jnp.float32)
     )
-    grad_input = lax.psum(partial_input.astype(jnp.bfloat16), "section")[None]
+    grad_input = expand_spot(partial_input.astype(jnp.bfloat16))[None]
     grads_all = jnp.stack([query_grad, key_grad, value_grad], axis=1)
     group_part = lax.psum_scatter(
         jnp.einsum("tr,tcf->rcf", tokens, grads_all, preferred_element_type=jnp.float32).astype(

time: 381 us -> 372 us (0.976)
  waiting for transfers between devices: 189 us -> 181 us
    psum x1 -> x0, waiting for transfers between devices: 15.5 us -> none  [per_device(): grad_input = lax.psum(partial_input.astype(jnp.bfloat16), 'section')[None]]
    unnamed x8, waiting for transfers between devices: 73.8 us -> 79.7 us
    unnamed x34 -> x27, local copies, waits for them, and re-layouts: 12.8 us -> 10.8 us
where the time goes in v1:
time: 372 us; the launch traced here: 371 us
  waiting for transfers between devices  181 us (49%)
  matrix products  54.8 us (15%)
  other arithmetic  46.5 us (12%)
  local copies, waits for them, and re-layouts  39.5 us (11%)
  loops' own time  19.7 us (5%)
  between operations  15.1 us (4%)
  starting transfers between devices  13.8 us (4%)
    unnamed x8, waiting for transfers between devices  79.7 us
    ppermute x2, waiting for transfers between devices, shifted(): lax.ppermute(value, axis, [(source, source + steps) for source in range(l...  31.1 us
    scatter-add x6, other arithmetic, backward(): running.at[0, slot_rows].add(key_part).at[1, slot_rows].add(value_part)  27.2 us
    all_gather x1, waiting for transfers between devices, per_device(): lax.all_gather(w_value, 'dp', axis=0, tiled=True)  24.1 us
    all_gather x1, waiting for transfers between devices, per_device(): lax.all_gather(w_key, 'dp', axis=0, tiled=True)  21.1 us
    ppermute x1, waiting for transfers between devices, extended(): lax.ppermute(tail, axis, [(i, (i + 1) % count) for i in range(ends)])  14.1 us
    dot_general x6, matrix products, attend(): jnp.einsum('qhd,skhd->hqsk', query_block, key_window, preferred_element_t...  12.4 us
    all_gather x1, waiting for transfers between devices, per_device(): lax.all_gather(w_query, 'dp', axis=0, tiled=True)  11.3 us
  transfers between devices with their start and end apart: 10, of which 7 were waited for; matrix products, arithmetic and copies ran while one was open for 10% of the time, Pallas kernels for 0%

profile of v1, /device:TPU:0, one launch (start us, length us, event | category | flops | bytes accessed | tf_op | source)
XLA Modules:
  0.0 370.7 jit_solution(15879130323404674931)
XLA Ops:
  9.5 24.1 %all-gather.8.cloned.1.call-done = bf16[1024,512]{1,0:T(8,128)(2,1)} async-done(((bf16[512,512]{1,0:T(8,128)(2,1)}), bf16[1024,512]{1,0:T(8,128)(2,1)}) %all-gather.8.cloned.1.call-update) | async-done | bytes 1048592 | tf_op jit(solution)/shard_map/all_gather | solution.py:60
  35.4 21.1 %all-gather.6.cloned.1.call-done = bf16[1024,512]{1,0:T(8,128)(2,1)} async-done(((bf16[512,512]{1,0:T(8,128)(2,1)}), bf16[1024,512]{1,0:T(8,128)(2,1)}) %all-gather.6.cloned.1.call-update) | async-done | bytes 1048592 | tf_op jit(solution)/shard_map/all_gather | solution.py:59
  60.4 5.4 %collective-permute-start = (bf16[2,384,512]{2,1,0:T(8,128)(2,1)S(1)}, bf16[2,384,512]{2,1,0:T(8,128)(2,1)}, u32[]{:S(2)}, u32[]{:S(2)}) collective-permute-start(bf16[2,384,512]{2,1,0:T(8,128)(2,1)S(1)} %pad_maximum_fusion.1), channel_id=1, source_target_pairs={{0,4},{4,8},{8,12},{12,16},{16,20},{20,24},{24,28},{1,5},{5,9},{9,... | collective-permute-start | bytes 2359304 | tf_op jit(solution)/shard_map/ppermute | solution.py:20
  68.1 11.3 %all-gather.10.cloned.1.call-done = bf16[1024,512]{1,0:T(8,128)(2,1)} async-done(((bf16[512,512]{1,0:T(8,128)(2,1)}), bf16[1024,512]{1,0:T(8,128)(2,1)}) %all-gather.10.cloned.1.call-update) | async-done | bytes 1048592 | tf_op jit(solution)/shard_map/all_gather | solution.py:58
  82.9 14.1 %collective-permute-done = bf16[2,384,512]{2,1,0:T(8,128)(2,1)} collective-permute-done((bf16[2,384,512]{2,1,0:T(8,128)(2,1)S(1)}, bf16[2,384,512]{2,1,0:T(8,128)(2,1)}, u32[]{:S(2)}, u32[]{:S(2)}) %collective-permute-start) | collective-permute-done | bytes 786464 | tf_op jit(solution)/shard_map/ppermute | solution.py:20
  98.8 4.6 %reshape.201 = bf16[2,9,128,8,64]{4,3,2,1,0:T(8,128)(2,1)} reshape(bf16[2,1152,512]{2,1,0:T(8,128)(2,1)S(1)} %pad_maximum_fusion) | data formatting | bytes 4718592 | tf_op jit(solution)/shard_map/reshape | solution.py:68
  103.3 6.1 %copy.83 = bf16[2,9,128,8,64]{2,4,1,3,0:T(8,128)(2,1)} copy(bf16[2,9,128,8,64]{4,3,2,1,0:T(8,128)(2,1)} %reshape.201) | data formatting | bytes 4718592 | tf_op jit(solution)/shard_map/while | solution.py:97
  109.5 2.8 broadcast_in_dim.61
  112.3 76.9 %while.27 = (s32[]{:T(128)}, f32[2,9,128,8,64]{2,4,3,1,0:T(8,128)}, bf16[3,128,8,64]{1,3,2,0:T(8,128)(2,1)S(1)}, s32[3]{0:T(128)S(1)}, s32[3,7]{1,0:T(4,128)S(1)...) while((s32[]{:T(128)}, f32[2,9,128,8,64]{2,4,3,1,0:T(8,128)}, ...), condition=%wide.region_10.11_spmd, body=%wide.region_4.10_spmd.sunk | while | flops 611644544 | bytes 56669256 | solution.py:129
  121.1 2.6 multiply_reduce_fusion.2
  128.9 4.8 %scatter_fusion = f32[2,9,128,8,64]{2,4,3,1,0:T(8,128)} fusion(f32[2,9,128,8,64]{2,4,3,1,0:T(8,128)} %get-tuple-element.398, s32[7]{0:T(128)S(1)} %select_bitcast_fusion.5, f32[7,128,8,64]{1,3,2,0:T(8,128)} %copy.129), kind=kCustom, calls=%fused_computation.clone.1 | custom fusion | flops 458752 | bytes 5505080 | tf_op jit(solution)/shard_map/while/body/eval_jaxpr/scatter-add | solution.py:125
  133.7 4.3 %scatter_fusion.1 = f32[2,9,128,8,64]{2,4,3,1,0:T(8,128)} fusion(f32[2,9,128,8,64]{2,4,3,1,0:T(8,128)} %scatter_fusion, s32[7]{0:T(128)S(1)} %get-tuple-element.349, f32[7,128,8,64]{1,3,2,0:T(8,128)S(1)} %copy.130), kind=kCustom, calls=%fused_computation.1.clone.1 | custom fusion | flops 458752 | bytes 5505080 | tf_op jit(solution)/shard_map/while/body/eval_jaxpr/scatter-add | solution.py:125
  146.8 2.6 multiply_reduce_fusion.2
  154.5 4.8 %scatter_fusion = f32[2,9,128,8,64]{2,4,3,1,0:T(8,128)} fusion(f32[2,9,128,8,64]{2,4,3,1,0:T(8,128)} %get-tuple-element.398, s32[7]{0:T(128)S(1)} %select_bitcast_fusion.5, f32[7,128,8,64]{1,3,2,0:T(8,128)} %copy.129), kind=kCustom, calls=%fused_computation.clone.1 | custom fusion | flops 458752 | bytes 5505080 | tf_op jit(solution)/shard_map/while/body/eval_jaxpr/scatter-add | solution.py:125
  159.4 4.2 %scatter_fusion.1 = f32[2,9,128,8,64]{2,4,3,1,0:T(8,128)} fusion(f32[2,9,128,8,64]{2,4,3,1,0:T(8,128)} %scatter_fusion, s32[7]{0:T(128)S(1)} %get-tuple-element.349, f32[7,128,8,64]{1,3,2,0:T(8,128)S(1)} %copy.130), kind=kCustom, calls=%fused_computation.1.clone.1 | custom fusion | flops 458752 | bytes 5505080 | tf_op jit(solution)/shard_map/while/body/eval_jaxpr/scatter-add | solution.py:125
  172.4 2.6 multiply_reduce_fusion.2
  180.2 4.8 %scatter_fusion = f32[2,9,128,8,64]{2,4,3,1,0:T(8,128)} fusion(f32[2,9,128,8,64]{2,4,3,1,0:T(8,128)} %get-tuple-element.398, s32[7]{0:T(128)S(1)} %select_bitcast_fusion.5, f32[7,128,8,64]{1,3,2,0:T(8,128)} %copy.129), kind=kCustom, calls=%fused_computation.clone.1 | custom fusion | flops 458752 | bytes 5505080 | tf_op jit(solution)/shard_map/while/body/eval_jaxpr/scatter-add | solution.py:125
  185.0 4.2 %scatter_fusion.1 = f32[2,9,128,8,64]{2,4,3,1,0:T(8,128)} fusion(f32[2,9,128,8,64]{2,4,3,1,0:T(8,128)} %scatter_fusion, s32[7]{0:T(128)S(1)} %get-tuple-element.349, f32[7,128,8,64]{1,3,2,0:T(8,128)S(1)} %copy.130), kind=kCustom, calls=%fused_computation.1.clone.1 | custom fusion | flops 458752 | bytes 5505080 | tf_op jit(solution)/shard_map/while/body/eval_jaxpr/scatter-add | solution.py:125
  189.2 2.8 bitcast_convert_fusion
  193.0 5.4 %collective-permute-start.2 = (bf16[2,3,128,512]{2,3,1,0:T(8,128)(2,1)}, bf16[2,3,128,512]{2,3,1,0:T(8,128)(2,1)}, u32[]{:S(2)}, u32[]{:S(2)}) collective-permute-start(bf16[2,3,128,512]{2,3,1,0:T(8,128)(2,1)} %get-tuple-element.236), channel_id=1, source_target_pairs={{0,4},{4,8},{8,12},{12,16},{16,20},{20,24},{24,28},{1,5},{5,9},{9,... | collective-permute-start | bytes 2359304 | tf_op jit(solution)/shard_map/ppermute | solution.py:32
  200.6 31.1 %collective-permute-done.2 = bf16[2,3,128,512]{2,3,1,0:T(8,128)(2,1)} collective-permute-done((bf16[2,3,128,512]{2,3,1,0:T(8,128)(2,1)}, bf16[2,3,128,512]{2,3,1,0:T(8,128)(2,1)}, u32[]{:S(2)}, u32[]{:S(2)}) %collective-permute-start.2) | collective-permute-done | bytes 786464 | tf_op jit(solution)/shard_map/ppermute | solution.py:32
  231.6 2.1 fusion.41
  235.3 4.5 %convolution_convert_fusion = bf16[3,512,1024]{2,1,0:T(8,128)(2,1)} fusion(bf16[384,1,512]{0,2,1:T(8,128)(2,1)} %copy.97, bf16[384,1,512]{0,2,1:T(8,128)(2,1)S(1)} %copy.96, bf16[384,1,512]{0,2,1:T(8,128)(2,1)S(1)} %stack_reshape.3, bf16[1,384,1024]{2,1,0:T(8,128)(2,1)S(1)} %copy-done), kind=kOutput, calls=%fused_computation.64 | convolution fusion | flops 1210712064 | bytes 5111808 | tf_op jit(solution)/shard_map/tr,tcf->rcf/dot_general | solution.py:153
  239.8 4.7 %copy.120 = bf16[1024,1536]{1,0:T(8,128)(2,1)} copy(bf16[1024,1536]{0,1:T(8,128)(2,1)} %bitcast.204) | data formatting | bytes 6291456
  250.1 68.9 %reduce-scatter.4.cloned.1.call-done = bf16[128,1536]{1,0:T(8,128)(2,1)} async-done(((bf16[1024,1536]{1,0:T(8,128)(2,1)}), bf16[128,1536]{1,0:T(8,128)(2,1)}) %reduce-scatter.4.cloned.1.call-update) | async-done | bytes 393232
  321.5 27.2 %while.26 = (s32[]{:T(128)}, bf16[3,128,8,64]{1,3,2,0:T(8,128)(2,1)S(1)}, s32[3]{0:T(128)S(1)}, bf16[2,9,128,8,64]{2,4,1,3,0:T(8,128)(2,1)}, s32[3,7]{1,0:T(4,12...) while((s32[]{:T(128)}, ...), condition=%wide.region_3.4_spmd, body=%wide.region_0.3_spmd.sunk | while | flops 245954576 | bytes 13128970 | solution.py:97
  325.4 2.1 select_reduce_fusion.4
  328.3 2.4 fusion.81
  337.3 2.4 fusion.81
  346.3 2.4 fusion.81
  350.4 2.9 reduce_sum.39
  353.2 8.7 %all-reduce.6.cloned.1.call-done = bf16[128,3,512]{2,1,0:T(4,128)(2,1)} async-done(((bf16[128,3,512]{2,1,0:T(4,128)(2,1)}), bf16[128,3,512]{2,1,0:T(4,128)(2,1)}) %all-reduce.6.cloned.1.call-update) | async-done | bytes 393232
  (117 shorter events, 71.3 us)
Async XLA Ops:
  7.2 26.4 %copy-start = (bf16[1,384,1024]{2,1,0:T(8,128)(2,1)S(1)}, bf16[1,384,1024]{2,1,0:T(8,128)(2,1)}, u32[]{:S(2)}) copy-start(bf16[1,384,1024]{2,1,0:T(8,128)(2,1)} %param.18) | copy-start | bytes 2359300
  7.2 26.4 %all-gather.8.cloned.1.call-start = ((), (), s32[]{:S(2)}) async-start(), calls=%async_computation.2 | async-start | bytes 1572864 | tf_op jit(solution)/shard_map/all_gather | solution.py:60
  7.9 48.6 %all-gather.6.cloned.1.call-start = ((), (), s32[]{:S(2)}) async-start(), calls=%async_computation.1 | async-start | bytes 1572864 | tf_op jit(solution)/shard_map/all_gather | solution.py:59
  8.7 57.2 %copy-start.7 = (s32[24,7]{0,1:T(8,128)S(1)}, s32[24,7]{0,1:T(8,128)}, u32[]{:S(2)}) copy-start(s32[24,7]{0,1:T(8,128)} %param.22) | copy-start | bytes 2020
  8.7 57.3 %copy-start.6 = (bf16[1,384,512]{2,1,0:T(8,128)(2,1)S(1)}, bf16[1,384,512]{2,1,0:T(8,128)(2,1)}, u32[]{:S(2)}) copy-start(bf16[1,384,512]{2,1,0:T(8,128)(2,1)} %param.23) | copy-start | bytes 1179652
  8.7 70.7 %all-gather.10.cloned.1.call-start = ((), (), s32[]{:S(2)}) async-start(), calls=%async_computation.3 | async-start | bytes 1572864 | tf_op jit(solution)/shard_map/all_gather | solution.py:58
  9.4 309.6 %reduce-scatter.4.cloned.1.call-start = ((), (), s32[]{:S(2)}) async-start(), calls=%async_computation.5 | async-start | bytes 3538944
  35.4 30.4 %copy-start.1 = (bf16[1,384,512]{2,1,0:T(8,128)(2,1)}, bf16[1,384,512]{2,1,0:T(8,128)(2,1)S(1)}, u32[]{:S(2)}) copy-start(bf16[1,384,512]{2,1,0:T(8,128)(2,1)S(1)} %fusion.43) | copy-start | bytes 1179652
  58.3 0.7 copy-start.2
  59.1 22.9 %collective-permute-start.1 = (bf16[2,384,512]{2,1,0:T(8,128)(2,1)S(1)}, bf16[2,384,512]{2,1,0:T(8,128)(2,1)S(1)}, u32[]{:S(2)}, u32[]{:S(2)}) collective-permute-start(bf16[2,384,512]{2,1,0:T(8,128)(2,1)S(1)} %pad_maximum_fusion.1), channel_id=1, source_target_pairs={{4,0},{8,4},{12,8},{16,12},{20,16},{24,20},{28,24},{5,1},{9,5},{13... | collective-permute-start | bytes 2359304 | tf_op jit(solution)/shard_map/ppermute | solution.py:22
  60.4 36.6 %collective-permute-start = (bf16[2,384,512]{2,1,0:T(8,128)(2,1)S(1)}, bf16[2,384,512]{2,1,0:T(8,128)(2,1)}, u32[]{:S(2)}, u32[]{:S(2)}) collective-permute-start(bf16[2,384,512]{2,1,0:T(8,128)(2,1)S(1)} %pad_maximum_fusion.1), channel_id=1, source_target_pairs={{0,4},{4,8},{8,12},{12,16},{16,20},{20,24},{24,28},{1,5},{5,9},{9,... | collective-permute-start | bytes 2359304 | tf_op jit(solution)/shard_map/ppermute | solution.py:20
  82.1 0.9 copy-start.5
  109.5 2.9 copy-start.8
  193.0 38.6 %collective-permute-start.2 = (bf16[2,3,128,512]{2,3,1,0:T(8,128)(2,1)}, bf16[2,3,128,512]{2,3,1,0:T(8,128)(2,1)}, u32[]{:S(2)}, u32[]{:S(2)}) collective-permute-start(bf16[2,3,128,512]{2,3,1,0:T(8,128)(2,1)} %get-tuple-element.236), channel_id=1, source_target_pairs={{0,4},{4,8},{8,12},{12,16},{16,20},{20,24},{24,28},{1,5},{5,9},{9,... | collective-permute-start | bytes 2359304 | tf_op jit(solution)/shard_map/ppermute | solution.py:32
  198.4 33.3 %collective-permute-start.3 = (bf16[2,3,128,512]{2,3,1,0:T(8,128)(2,1)S(1)}, bf16[2,3,128,512]{2,3,1,0:T(8,128)(2,1)}, u32[]{:S(2)}, u32[]{:S(2)}) collective-permute-start(bf16[2,3,128,512]{2,3,1,0:T(8,128)(2,1)S(1)} %get-tuple-element.237), channel_id=1, source_target_pairs={{4,0},{8,4},{12,8},{16,12},{20,16},{24,20},{28,24},{5,1},{9,5},{13... | collective-permute-start | bytes 2359304 | tf_op jit(solution)/shard_map/ppermute | solution.py:32
  244.5 2.1 copy-start.3
  244.5 105.8 %all-gather.12.cloned.1.call-start = ((), (), s32[]{:S(2)}) async-start(), calls=%async_computation.4 | async-start | bytes 2359296 | tf_op jit(solution)/shard_map/all_gather | solution.py:9
  244.6 2.6 copy-start.4
  247.2 1.6 copy-start.9
  248.8 113.1 %all-reduce.6.cloned.1.call-start = ((), (), s32[]{:S(2)}) async-start(), calls=%async_computation.6 | async-start | bytes 1048576
Sparse Core Ops, SparseCore 0:
  9.6 23.9 all-gather.7
  35.1 21.2 all-gather.5
  58.0 21.2 all-gather.9
  244.7 74.2 reduce-scatter.3
  321.0 8.9 all-gather.11
  332.1 29.7 all-reduce.5
